TPU v7x, 128 devices: a whole 4x4x4 slice. The times are simulated.
128 devices in a mesh: req: 8 (over x, core), kv: 16 (over y, z).
Axes of the slice: x: 4, y: 4, z: 4, core: 2. Of those that a mesh axis runs over, the one named last changes fastest.
Arguments:
- x_steps: bfloat16 [4, 1024, 1536], P(None, ('req', 'kv')), may hold values from -6 to 6
- lengths: int32 [128], replicated, may hold values from 16 to 8192
- perm: int32 [128], replicated, may hold values from 0 to 127, as said below
- parents: int32 [4, 1024], replicated, may hold values from 0 to 7
- table: int32 [1024, 9], P(('req', 'kv')), may hold values from 0 to 9215, as said below
- pool: bfloat16 [9216, 128, 256], P(('req', 'kv')), may hold values from -900 to 900
- norm_attn: float32 [1536], replicated, may hold values from 0.1 to 1.9
- w_query: bfloat16 [1536, 1536], replicated, may hold values from -0.15625 to 0.15625
- w_keyval: bfloat16 [1536, 256], replicated, may hold values from -0.15625 to 0.15625
- w_out: bfloat16 [1536, 1536], replicated, may hold values from -0.15625 to 0.15625
- norm_mlp: float32 [1536], replicated, may hold values from 0.1 to 1.9
- w_gate: bfloat16 [1536, 4608], P(None, 'kv'), may hold values from -0.15625 to 0.15625
- w_up: bfloat16 [1536, 4608], P(None, 'kv'), may hold values from -0.15625 to 0.15625
- w_down: bfloat16 [4608, 1536], P('kv'), may hold values from -0.09375 to 0.09375
Outputs:
- outputs: bfloat16 [4, 1024, 1536], P(None, ('req', 'kv'))
Inputs may be any that keep to these rules, and one draw needn't show every extreme that they name: perm is a permutation with perm[s] % 16 == s % 16; among the 8 slots s with one s // 16 and one s % 16 // 8, every req index occurs as perm[s] // 16 exactly once. The entries of row b lie in [(b // 8) * 72, (b // 8 + 1) * 72); no page appears twice in the table.
All inputs are finite; a program needn't handle non-finite values.
Results may differ from a plain program's by a relative error of at most 0.02.
Values may be sent and summed in bfloat16 or wider, within the bound.
No kernel may reach another device: no remote copies, remote signals or barrier semaphores. Data moves between devices by JAX's collectives and lax.ppermute only.
A program may use at most 192 MiB of HBM per device.

v0:
```python
import jax
import jax.numpy as jnp
from jax import lax
from jax.sharding import PartitionSpec as P

WINDOW = 1024
PAGE = 128
BEAMS = 8
EPSILON = 1e-06
NEGATIVE = -1e30


def merged_2(array, axis, combine):
    everything = jax.tree.map(lambda part: lax.all_gather(part, axis), array)
    first = jax.tree.map(lambda part: part[0], everything)

    def turn(k, so_far):
        return combine(so_far, jax.tree.map(lambda part: part[k], everything))

    return lax.fori_loop(1, lax.axis_size(axis), turn, first)


def member_of(beam_index, half_index, halves):
    return beam_index % 2 + 2 * half_index + 2 * halves * (beam_index // 2)


def rms_round(values, gain):
    wide = values.astype(jnp.float32)
    mean_square = jnp.mean(wide * wide, axis=-1, keepdims=True)
    return (wide * lax.rsqrt(mean_square + EPSILON) * gain).astype(jnp.bfloat16)


def page_partial(queries, pages, key_pos, length, step_index):
    head_dim = queries.shape[-1]
    keys = pages[:, :, :head_dim]
    values = pages[:, :, head_dim:]
    scores = jnp.einsum(
        "jrhd,rkd->jrhk", queries, keys, preferred_element_type=jnp.float32
    ) * head_dim ** (-0.5)
    allowed = (key_pos < length[:, None]) & (key_pos > length[:, None] + step_index - WINDOW)
    scores = jnp.where(allowed[None, :, None, :], scores, NEGATIVE)
    highest = jnp.max(scores, axis=-1)
    weights = jnp.exp(scores - highest[..., None]).astype(jnp.bfloat16)
    totals = jnp.sum(weights.astype(jnp.float32), axis=-1)
    weighted = jnp.einsum("jrhk,rkd->jrhd", weights, values, preferred_element_type=jnp.float32)
    return (highest, totals, weighted)


def fresh_partial(queries, entries, count):
    head_dim = queries.shape[-1]
    keys = entries[..., :count, :head_dim]
    values = entries[..., :count, head_dim:]
    scores = jnp.einsum(
        "...hd,...kd->...hk", queries, keys, preferred_element_type=jnp.float32
    ) * head_dim ** (-0.5)
    highest = jnp.max(scores, axis=-1)
    weights = jnp.exp(scores - highest[..., None]).astype(jnp.bfloat16)
    totals = jnp.sum(weights.astype(jnp.float32), axis=-1)
    weighted = jnp.einsum("...hk,...kd->...hd", weights, values, preferred_element_type=jnp.float32)
    return (highest, totals, weighted)


def join_parts(first, second):
    highest = jnp.maximum(first[0], second[0])
    scale_first = jnp.exp(first[0] - highest)
    scale_second = jnp.exp(second[0] - highest)
    totals = first[1] * scale_first + second[1] * scale_second
    weighted = first[2] * scale_first[..., None] + second[2] * scale_second[..., None]
    return (highest, totals, weighted)


def feed_forward(mlp_in, w_gate, w_up, w_down):
    gate = jnp.dot(mlp_in, w_gate, preferred_element_type=jnp.float32)
    upward = jnp.dot(mlp_in, w_up, preferred_element_type=jnp.float32)
    hidden = (jax.nn.gelu(gate, approximate=True) * upward).astype(jnp.bfloat16)
    return jnp.dot(hidden, w_down, preferred_element_type=jnp.float32)


def rank_within(labels, offsets):
    earlier = (labels[None, :] == labels[:, None]) & (offsets[None, :] < offsets[:, None])
    return jnp.sum(earlier.astype(jnp.int32), axis=1)


def pick_half(array, halves, half):
    shaped = array.reshape((BEAMS // 2, halves, 2) + array.shape[1:])
    picked = lax.dynamic_index_in_dim(shaped, half, 1, keepdims=False)
    return picked.reshape((BEAMS,) + array.shape[1:])


def place_block(block, filler, halves, half):
    whole = jnp.full((BEAMS // 2, halves, 2) + block.shape[1:], filler, block.dtype)
    placed = lax.dynamic_update_slice_in_dim(
        whole, block.reshape((BEAMS // 2, 1, 2) + block.shape[1:]), half, 1
    )
    return placed.reshape((BEAMS * halves,) + block.shape[1:])


def on_device(
    x_steps,
    lengths,
    perm,
    parents,
    table,
    pool,
    norm_attn,
    w_query,
    w_keyval,
    w_out,
    norm_mlp,
    w_gate,
    w_up,
    w_down,
):
    steps, rows, width = x_steps.shape
    head_dim = pool.shape[2] // 2
    heads = w_query.shape[1] // head_dim
    span = table.shape[1] * pool.shape[1]
    req_count = lax.axis_size("req")
    kv_count = lax.axis_size("kv")
    group = lax.axis_index("req")
    member = lax.axis_index("kv")
    halves = kv_count // BEAMS
    half = member // 2 % halves
    beam = member % 2 + 2 * (member // (2 * halves))
    per_group = halves * rows
    group_rows = kv_count * rows
    quota = rows // req_count
    offsets = jnp.arange(rows, dtype=jnp.int32)
    slot_ids = group * per_group + half * rows + offsets
    placed = lax.dynamic_slice_in_dim(perm.reshape(req_count, per_group), half * rows, rows, 1)
    serving = lax.dynamic_index_in_dim(placed, group, 0, keepdims=False)
    target = jnp.sum(
        jnp.where(placed == slot_ids[None, :], jnp.arange(req_count, dtype=jnp.int32)[:, None], 0),
        axis=0,
    )
    anchor = serving // per_group
    send_order = jnp.argsort(target * rows + offsets)
    outgoing = x_steps[:, send_order].reshape(steps, req_count, quota, width)
    arrived = lax.all_to_all(outgoing, "req", split_axis=1, concat_axis=1, tiled=True).reshape(
        steps, rows, width
    )
    inputs = arrived[:, anchor * quota + rank_within(anchor, offsets)]
    length = lengths[serving]
    first_page = jnp.maximum(length - WINDOW + 1, 0) // PAGE
    key_pos = first_page[:, None] * PAGE + jnp.arange(span, dtype=jnp.int32)[None, :]
    device = group * kv_count + member
    pages = pool[table - device * pool.shape[0]].reshape(rows, span, 2 * head_dim)
    family = lax.dynamic_slice_in_dim(parents, group * group_rows, group_rows, 1)
    row_ids = jnp.arange(group_rows, dtype=jnp.int32)
    row_member = row_ids // rows
    row_half = row_member // 2 % halves
    within = row_ids % rows
    ancestor = row_member % 2 + 2 * (row_member // (2 * halves))
    recent = jnp.zeros((group_rows, steps, 2 * head_dim), jnp.bfloat16)
    results = []
    for step_index in range(steps):
        parent_rows = member_of(family[step_index], row_half, halves) * rows + within
        ancestor = ancestor[parent_rows]
        recent = recent[parent_rows]
        current = inputs[step_index]
        normed = rms_round(current, norm_attn)
        query = jnp.dot(normed, w_query, preferred_element_type=jnp.float32).astype(jnp.bfloat16)
        fresh = jnp.dot(normed, w_keyval, preferred_element_type=jnp.float32).astype(jnp.bfloat16)
        query_all, fresh_all = (
            lax.all_gather(query, "kv", axis=0, tiled=True),
            lax.all_gather(fresh, "kv", axis=0, tiled=True),
        )
        recent = recent.at[:, step_index].set(fresh_all)
        query_block = pick_half(query_all.reshape(kv_count, rows, heads, head_dim), halves, half)
        held = pick_half(ancestor.reshape(kv_count, rows), halves, half) == beam
        page = page_partial(query_block, pages, key_pos, length, step_index)
        held_heads = held[..., None]
        highest = place_block(jnp.where(held_heads, page[0], NEGATIVE), NEGATIVE, halves, half)
        totals = place_block(jnp.where(held_heads, page[1], 0.0), 0.0, halves, half)
        weighted = place_block(jnp.where(held_heads[..., None], page[2], 0.0), 0.0, halves, half)
        merged = merged_2((highest, totals, weighted), "kv", join_parts)
        page_own = tuple(
            (
                lax.dynamic_index_in_dim(member_part, member, 0, keepdims=False)
                for member_part in merged
            )
        )
        own_entries = lax.dynamic_slice_in_dim(recent, member * rows, rows, 0)
        joined = join_parts(
            page_own,
            fresh_partial(query.reshape(rows, heads, head_dim), own_entries, step_index + 1),
        )
        attended = (
            (joined[2] / joined[1][..., None]).astype(jnp.bfloat16).reshape(rows, heads * head_dim)
        )
        residual = (
            current.astype(jnp.float32)
            + jnp.dot(attended, w_out, preferred_element_type=jnp.float32)
        ).astype(jnp.bfloat16)
        terms = feed_forward(
            lax.all_gather(rms_round(residual, norm_mlp), "kv", axis=0, tiled=True),
            w_gate,
            w_up,
            w_down,
        )
        summed = lax.psum_scatter(
            terms.astype(jnp.bfloat16), "kv", scatter_dimension=0, tiled=True
        ).astype(jnp.float32)
        results.append((residual.astype(jnp.float32) + summed).astype(jnp.bfloat16))
    finished = jnp.stack(results)
    back_order = jnp.argsort(anchor * rows + offsets)
    leaving = finished[:, back_order].reshape(steps, req_count, quota, width)
    returned = lax.all_to_all(leaving, "req", split_axis=1, concat_axis=1, tiled=True).reshape(
        steps, rows, width
    )
    return returned[:, target * quota + rank_within(target, offsets)]


def solution(mesh):
    in_specs = (
        P(None, ("req", "kv"), None),
        P(),
        P(),
        P(),
        P(("req", "kv"), None),
        P(("req", "kv"), None, None),
        P(),
        P(),
        P(),
        P(),
        P(),
        P(None, "kv"),
        P(None, "kv"),
        P("kv", None),
    )
    out_specs = P(None, ("req", "kv"), None)
    return jax.shard_map(
        on_device, mesh=mesh, in_specs=in_specs, out_specs=out_specs, check_vma=False
    )
```

profile of v0, /device:TPU:1, one launch (start us, length us, event | category | flops | bytes accessed | tf_op | source)
XLA Modules:
  0.0 938.8 jit_solution(8522241222401222963)
XLA Ops:
  12.4 5.8 all-to-all-start
  27.0 7.8 gather_fusion.4
  35.8 3.2 convolution_convert_fusion.4
  39.0 20.2 %all_gather.90 = bf16[128,1536]{1,0:T(8,128)(2,1)S(1)} all-gather(bf16[8,1536]{1,0:T(8,128)(2,1)S(1)} %convolution_convert_fusion.4), channel_id=1, replica_groups=mesh['req'=8,'kv'=16] {'kv'}, dimensions={0}, use_global_device_ids=true | all-gather | bytes 417792 | tf_op jit(solution)/shard_map/all_gather | solution.py:165
  64.0 3.1 convolution_convert_fusion.7
  67.1 19.5 %all_gather.72 = bf16[128,1536]{1,0:T(8,128)(2,1)S(1)} all-gather(bf16[8,1536]{1,0:T(8,128)(2,1)S(1)} %convolution_convert_fusion.7), channel_id=1, replica_groups=mesh['req'=8,'kv'=16] {'kv'}, dimensions={0}, use_global_device_ids=true | all-gather | bytes 417792 | tf_op jit(solution)/shard_map/all_gather | solution.py:165
  86.7 2.8 bitcast_reduce_fusion.3
  93.2 3.1 convolution_convert_fusion.6
  96.3 17.8 %all_gather.78 = bf16[128,1536]{1,0:T(8,128)(2,1)S(1)} all-gather(bf16[8,1536]{1,0:T(8,128)(2,1)S(1)} %convolution_convert_fusion.6), channel_id=1, replica_groups=mesh['req'=8,'kv'=16] {'kv'}, dimensions={0}, use_global_device_ids=true | all-gather | bytes 417792 | tf_op jit(solution)/shard_map/all_gather | solution.py:165
  114.2 2.9 bitcast_reduce_fusion.2
  121.7 3.4 convert_reduce_fusion
  125.7 20.9 %all_gather.76 = bf16[128,256]{1,0:T(8,128)(2,1)S(1)} all-gather(bf16[8,256]{1,0:T(8,128)(2,1)S(1)} %convolution_convert_fusion.11), channel_id=1, replica_groups=mesh['req'=8,'kv'=16] {'kv'}, dimensions={0}, use_global_device_ids=true | all-gather | bytes 69632 | tf_op jit(solution)/shard_map/all_gather | solution.py:166
  149.5 16.4 %all_gather.82 = bf16[128,256]{1,0:T(8,128)(2,1)S(1)} all-gather(bf16[8,256]{1,0:T(8,128)(2,1)S(1)} %convolution_convert_fusion.10), channel_id=1, replica_groups=mesh['req'=8,'kv'=16] {'kv'}, dimensions={0}, use_global_device_ids=true | all-gather | bytes 69632 | tf_op jit(solution)/shard_map/all_gather | solution.py:166
  168.9 19.8 %all_gather.88 = bf16[128,256]{1,0:T(8,128)(2,1)S(1)} all-gather(bf16[8,256]{1,0:T(8,128)(2,1)S(1)} %convolution_convert_fusion.9), channel_id=1, replica_groups=mesh['req'=8,'kv'=16] {'kv'}, dimensions={0}, use_global_device_ids=true | all-gather | bytes 69632 | tf_op jit(solution)/shard_map/all_gather | solution.py:166
  191.6 16.4 %all_gather.94 = bf16[128,256]{1,0:T(8,128)(2,1)S(1)} all-gather(bf16[8,256]{1,0:T(8,128)(2,1)S(1)} %convolution_convert_fusion.8), channel_id=1, replica_groups=mesh['req'=8,'kv'=16] {'kv'}, dimensions={0}, use_global_device_ids=true | all-gather | bytes 69632 | tf_op jit(solution)/shard_map/all_gather | solution.py:166
  208.1 3.4 convert_reduce_fusion.3
  211.9 3.4 convert_reduce_fusion.2
  215.7 3.2 convolution_convert_fusion.5
  218.9 21.9 %all_gather.84 = bf16[128,1536]{1,0:T(8,128)(2,1)S(1)} all-gather(bf16[8,1536]{1,0:T(8,128)(2,1)S(1)} %convolution_convert_fusion.5), channel_id=1, replica_groups=mesh['req'=8,'kv'=16] {'kv'}, dimensions={0}, use_global_device_ids=true | all-gather | bytes 417792 | tf_op jit(solution)/shard_map/all_gather | solution.py:165
  240.9 2.7 bitcast_reduce_fusion.1
  248.8 20.0 %all_gather.91 = f32[16,16,8,12]{1,2,3,0:T(8,128)} all-gather(f32[1,16,8,12]{1,2,3,0:T(8,128)S(1)} %copy.375), channel_id=1, replica_groups=mesh['req'=8,'kv'=16] {'kv'}, dimensions={0}, use_global_device_ids=true | all-gather | bytes 104448 | tf_op jit(solution)/shard_map/all_gather | solution.py:14
  268.8 22.4 %all_gather.92 = f32[16,16,8,12]{1,2,3,0:T(8,128)} all-gather(f32[1,16,8,12]{1,2,3,0:T(8,128)S(1)} %copy.378), channel_id=1, replica_groups=mesh['req'=8,'kv'=16] {'kv'}, dimensions={0}, use_global_device_ids=true | all-gather | bytes 104448 | tf_op jit(solution)/shard_map/all_gather | solution.py:14
  291.2 20.8 %all_gather.73 = f32[16,16,8,12]{1,2,3,0:T(8,128)S(1)} all-gather(f32[1,16,8,12]{1,2,3,0:T(8,128)S(1)} %copy.320), channel_id=1, replica_groups=mesh['req'=8,'kv'=16] {'kv'}, dimensions={0}, use_global_device_ids=true | all-gather | bytes 104448 | tf_op jit(solution)/shard_map/all_gather | solution.py:14
  312.0 22.6 %all_gather.74 = f32[16,16,8,12]{1,2,3,0:T(8,128)S(1)} all-gather(f32[1,16,8,12]{1,2,3,0:T(8,128)S(1)} %copy.323), channel_id=1, replica_groups=mesh['req'=8,'kv'=16] {'kv'}, dimensions={0}, use_global_device_ids=true | all-gather | bytes 104448 | tf_op jit(solution)/shard_map/all_gather | solution.py:14
  334.6 21.6 %all_gather.79 = f32[16,16,8,12]{1,2,3,0:T(8,128)S(1)} all-gather(f32[1,16,8,12]{1,2,3,0:T(8,128)S(1)} %copy.341), channel_id=1, replica_groups=mesh['req'=8,'kv'=16] {'kv'}, dimensions={0}, use_global_device_ids=true | all-gather | bytes 104448 | tf_op jit(solution)/shard_map/all_gather | solution.py:14
  356.3 18.0 %all_gather.80 = f32[16,16,8,12]{1,2,3,0:T(8,128)S(1)} all-gather(f32[1,16,8,12]{1,2,3,0:T(8,128)S(1)} %copy.344), channel_id=1, replica_groups=mesh['req'=8,'kv'=16] {'kv'}, dimensions={0}, use_global_device_ids=true | all-gather | bytes 104448 | tf_op jit(solution)/shard_map/all_gather | solution.py:14
  374.3 19.4 %all_gather.85 = f32[16,16,8,12]{1,2,3,0:T(8,128)} all-gather(f32[1,16,8,12]{1,2,3,0:T(8,128)S(1)} %copy.358), channel_id=1, replica_groups=mesh['req'=8,'kv'=16] {'kv'}, dimensions={0}, use_global_device_ids=true | all-gather | bytes 104448 | tf_op jit(solution)/shard_map/all_gather | solution.py:14
  393.7 20.4 %all_gather.86 = f32[16,16,8,12]{1,2,3,0:T(8,128)} all-gather(f32[1,16,8,12]{1,2,3,0:T(8,128)S(1)} %copy.361), channel_id=1, replica_groups=mesh['req'=8,'kv'=16] {'kv'}, dimensions={0}, use_global_device_ids=true | all-gather | bytes 104448 | tf_op jit(solution)/shard_map/all_gather | solution.py:14
  420.4 2.7 fusion.37
  426.7 46.2 %while.83 = (s32[]{:T(128)}, f32[16,8,12]{0,1,2:T(8,128)S(1)}, f32[16,8,12]{0,1,2:T(8,128)S(1)}, f32[16,8,12,128]{3,2,1,0:T(8,128)S(1)}, f32[16,16,8,12]{1,2,3,0...) while((s32[]{:T(128)}, f32[16,8,12]{0,1,2:T(8,128)S(1)}, ...), condition=%wide.region_32.33_spmd, body=%wide.region_31.32_spmd.sunk | while | flops 599045 | bytes 4018327 | solution.py:20
  475.2 46.3 %while.80 = (s32[]{:T(128)}, f32[16,8,12]{0,1,2:T(8,128)S(1)}, f32[16,8,12]{0,1,2:T(8,128)S(1)}, f32[16,8,12,128]{3,2,1,0:T(8,128)S(1)}, f32[16,16,8,12]{1,2,3,0...) while((s32[]{:T(128)}, f32[16,8,12]{0,1,2:T(8,128)S(1)}, ...), condition=%wide.region_7.8_spmd, body=%wide.region_6.7_spmd.sunk | while | flops 599045 | bytes 4018327 | solution.py:20
  524.6 73.6 %while.81 = (s32[]{:T(128)}, f32[16,8,12]{0,1,2:T(8,128)S(1)}, f32[16,8,12]{0,1,2:T(8,128)S(1)}, f32[16,8,12,128]{3,2,1,0:T(8,128)}, f32[16,16,8,12]{1,2,3,0:T(8...) while((s32[]{:T(128)}, f32[16,8,12]{0,1,2:T(8,128)S(1)}, ...), condition=%wide.region_14.15_spmd, body=%wide.region_13.14_spmd.sunk | while | flops 599045 | bytes 4018327 | solution.py:20
  531.8 2.6 fusion.302
  536.7 2.6 fusion.302
  556.4 2.6 fusion.302
  601.4 3.4 multiply_reduce_fusion.3
  604.8 3.2 multiply_reduce_fusion.2
  610.3 46.2 %while.82 = (s32[]{:T(128)}, f32[16,8,12]{0,1,2:T(8,128)S(1)}, f32[16,8,12]{0,1,2:T(8,128)S(1)}, f32[16,8,12,128]{3,2,1,0:T(8,128)S(1)}, f32[16,16,8,12]{1,2,3,0...) while((s32[]{:T(128)}, f32[16,8,12]{0,1,2:T(8,128)S(1)}, ...), condition=%wide.region_23.24_spmd, body=%wide.region_22.23_spmd.sunk | while | flops 599045 | bytes 4018327 | solution.py:20
  657.8 3.2 multiply_reduce_fusion.1
  661.8 16.6 %all_gather.95 = bf16[128,1536]{1,0:T(8,128)(2,1)S(1)} all-gather(bf16[8,1536]{1,0:T(8,128)(2,1)S(1)} %get-tuple-element.991), channel_id=1, replica_groups=mesh['req'=8,'kv'=16] {'kv'}, dimensions={0}, use_global_device_ids=true | all-gather | bytes 417792 | tf_op jit(solution)/shard_map/all_gather | solution.py:196
  678.4 17.7 %all_gather.89 = bf16[128,1536]{1,0:T(8,128)(2,1)S(1)} all-gather(bf16[8,1536]{1,0:T(8,128)(2,1)S(1)} %get-tuple-element.990), channel_id=1, replica_groups=mesh['req'=8,'kv'=16] {'kv'}, dimensions={0}, use_global_device_ids=true | all-gather | bytes 417792 | tf_op jit(solution)/shard_map/all_gather | solution.py:196
  698.1 3.0 convolution_convert_fusion
  701.2 2.8 convolution_convert_fusion.1
  703.9 16.3 %all_gather.83 = bf16[128,1536]{1,0:T(8,128)(2,1)S(1)} all-gather(bf16[8,1536]{1,0:T(8,128)(2,1)} %get-tuple-element.989), channel_id=1, replica_groups=mesh['req'=8,'kv'=16] {'kv'}, dimensions={0}, use_global_device_ids=true | all-gather | bytes 417792 | tf_op jit(solution)/shard_map/all_gather | solution.py:196
  722.6 17.9 %all_gather.77 = bf16[128,1536]{1,0:T(8,128)(2,1)S(1)} all-gather(bf16[8,1536]{1,0:T(8,128)(2,1)S(1)} %copy-done.28), channel_id=1, replica_groups=mesh['req'=8,'kv'=16] {'kv'}, dimensions={0}, use_global_device_ids=true | all-gather | bytes 417792 | tf_op jit(solution)/shard_map/all_gather | solution.py:196
  744.1 170.9 %all-reduce.7.cloned.1.call-done = (bf16[128,1536]{1,0:T(8,128)(2,1)}, bf16[128,1536]{1,0:T(8,128)(2,1)}, bf16[128,1536]{1,0:T(8,128)(2,1)}, bf16[128,1536]{1,0:T(8,128)(2,1)}) async-done(((bf16[128,1536]{1,0:T(8,128)(2,1)}, bf16[128,1536]{1,0:T(8,128)(2,1)}, bf16[128,1536]{1,0:T(8,128)(2,1)}, bf16[128,1536]{1,0:T(8,128)(2,1)}), (bf16[128,1536]{1,0:T(8,128)(2,1)}, bf16[128,1536]{1,0:T(8,128)(2,1)}, ...) | async-done | bytes 1572880
  919.3 6.5 all-to-all-start.1
  925.8 5.0 all-to-all-done.1
  (612 shorter events, 281.7 us)
Async XLA Ops:
  6.5 691.6 %copy-start = (bf16[288,1536]{1,0:T(8,128)(2,1)S(1)}, bf16[288,1536]{1,0:T(8,128)(2,1)}, u32[]{:S(2)}) copy-start(bf16[288,1536]{1,0:T(8,128)(2,1)} %param.43) | copy-start | bytes 2654212
  7.4 27.4 %copy-start.38 = (s32[8]{0:T(128)}, s32[8]{0:T(128)S(1)}, u32[]{:S(2)}) copy-start(s32[8]{0:T(128)S(1)} %select_reduce_fusion) | copy-start | bytes 100
  12.4 22.5 %all-to-all-start = ((bf16[4,8,1,1536]{3,0,2,1:T(4,128)(2,1)}), bf16[4,8,1,1536]{3,0,2,1:T(4,128)(2,1)S(1)}, u32[]{:S(2)}, u32[]{:S(2)}) async-start(bf16[4,8,1,1536]{3,0,2,1:T(4,128)(2,1)} %copy.313), calls=%async_computation | async-start | bytes 196608 | tf_op jit(solution)/shard_map/all_to_all | solution.py:139
  18.2 407.1 %all-gather.11.cloned.1.call-start = ((), (), s32[]{:S(2)}) async-start(), calls=%async_computation.5 | async-start | bytes 13369344 | tf_op jit(solution)/shard_map/all_gather | solution.py:14
  27.0 8.8 copy-start.22
  35.6 23.7 %copy-start.6 = (bf16[72,128,256]{2,1,0:T(8,128)(2,1)S(1)}, bf16[72,128,256]{2,1,0:T(8,128)(2,1)}, u32[]{:S(2)}) copy-start(bf16[72,128,256]{2,1,0:T(8,128)(2,1)} %gather_fusion.4) | copy-start | bytes 14155780
  60.4 2.2 copy-start.9
  63.7 409.4 %all-gather.5.cloned.1.call-start = ((), (), s32[]{:S(2)}) async-start(), calls=%async_computation.2 | async-start | bytes 13369344 | tf_op jit(solution)/shard_map/all_gather | solution.py:14
  67.1 22.4 %slice-start.2 = ((s8[4718592]{0:T(1024)(128)(4,1)}), s8[4194304]{0:T(1024)(128)(4,1)S(1)}, s32[]{:S(2)}) async-start(s8[4718592]{0:T(1024)(128)(4,1)} %bitcast.579), calls=%async_computation.9 | async-start | bytes 8388608
  86.7 2.8 slice-start.3
  89.5 2.2 copy-start.7
  92.9 429.2 %all-gather.7.cloned.1.call-start = ((), (), s32[]{:S(2)}) async-start(), calls=%async_computation.3 | async-start | bytes 13369344 | tf_op jit(solution)/shard_map/all_gather | solution.py:14
  96.3 20.7 %slice-start.4 = ((s8[4718592]{0:T(1024)(128)(4,1)}), s8[4194304]{0:T(1024)(128)(4,1)S(1)}, s32[]{:S(2)}) async-start(s8[4718592]{0:T(1024)(128)(4,1)} %bitcast.582), calls=%async_computation.11 | async-start | bytes 8388608
  114.2 2.9 slice-start.5
  118.3 7.2 copy-start.5
  120.4 488.5 %all-gather.9.cloned.1.call-start = ((), (), s32[]{:S(2)}) async-start(), calls=%async_computation.4 | async-start | bytes 13369344 | tf_op jit(solution)/shard_map/all_gather | solution.py:14
  167.8 246.9 %copy-start.21 = (bf16[128,4,256]{2,1,0:T(4,128)(2,1)}, bf16[128,4,256]{2,1,0:T(4,128)(2,1)S(1)}, u32[]{:S(2)}) copy-start(bf16[128,4,256]{2,1,0:T(4,128)(2,1)S(1)} %scatter.15) | copy-start | bytes 786436
  190.5 226.4 %copy-start.20 = (bf16[128,4,256]{2,1,0:T(4,128)(2,1)}, bf16[128,4,256]{2,1,0:T(4,128)(2,1)S(1)}, u32[]{:S(2)}) copy-start(bf16[128,4,256]{2,1,0:T(4,128)(2,1)S(1)} %scatter.16) | copy-start | bytes 786436
  248.7 169.2 %copy-start.27 = (bf16[128,4,256]{2,1,0:T(4,128)(2,1)}, bf16[128,4,256]{2,1,0:T(4,128)(2,1)S(1)}, u32[]{:S(2)}) copy-start(bf16[128,4,256]{2,1,0:T(4,128)(2,1)S(1)} %scatter.19) | copy-start | bytes 786436
  248.8 171.7 %copy-start.11 = (f32[8,1152,8,12]{1,3,2,0:T(8,128)S(1)}, f32[8,1152,8,12]{1,3,2,0:T(8,128)}, u32[]{:S(2)}) copy-start(f32[8,1152,8,12]{1,3,2,0:T(8,128)} %copy-done.10) | copy-start | bytes 10616836
  312.0 107.6 %copy-start.18 = (f32[16,16,8,12]{1,2,3,0:T(8,128)}, f32[16,16,8,12]{1,2,3,0:T(8,128)S(1)}, u32[]{:S(2)}) copy-start(f32[16,16,8,12]{1,2,3,0:T(8,128)S(1)} %all_gather.73) | copy-start | bytes 294916
  334.6 85.0 %copy-start.19 = (f32[16,16,8,12]{1,2,3,0:T(8,128)}, f32[16,16,8,12]{1,2,3,0:T(8,128)S(1)}, u32[]{:S(2)}) copy-start(f32[16,16,8,12]{1,2,3,0:T(8,128)S(1)} %all_gather.74) | copy-start | bytes 294916
  356.3 62.5 %copy-start.16 = (f32[16,16,8,12]{1,2,3,0:T(8,128)}, f32[16,16,8,12]{1,2,3,0:T(8,128)S(1)}, u32[]{:S(2)}) copy-start(f32[16,16,8,12]{1,2,3,0:T(8,128)S(1)} %all_gather.79) | copy-start | bytes 294916
  374.3 45.3 %copy-start.17 = (f32[16,16,8,12]{1,2,3,0:T(8,128)}, f32[16,16,8,12]{1,2,3,0:T(8,128)S(1)}, u32[]{:S(2)}) copy-start(f32[16,16,8,12]{1,2,3,0:T(8,128)S(1)} %all_gather.80) | copy-start | bytes 294916
  414.8 8.3 copy-start.37
  417.1 7.6 copy-start.29
  424.4 490.5 %all-reduce.7.cloned.1.call-start = ((), (), s32[]{:S(2)}) async-start(), calls=%async_computation.6 | async-start | bytes 3145728
  475.2 46.6 %copy-start.40 = (f32[8,1,12]{2,1,0:T(1,128)S(1)}, f32[8,1,12]{2,1,0:T(1,128)}, u32[]{:S(2)}) copy-start(f32[8,1,12]{2,1,0:T(1,128)} %fusion.132) | copy-start | bytes 1156
  524.5 73.9 %copy-start.34 = (f32[8,12]{1,0:T(8,128)S(1)}, f32[8,12]{1,0:T(8,128)}, u32[]{:S(2)}) copy-start(f32[8,12]{1,0:T(8,128)} %copy-done.33) | copy-start | bytes 1156
  524.5 73.9 %copy-start.35 = (f32[8,12]{1,0:T(8,128)S(1)}, f32[8,12]{1,0:T(8,128)}, u32[]{:S(2)}) copy-start(f32[8,12]{1,0:T(8,128)} %convert_reduce_fusion.6) | copy-start | bytes 1156
  601.4 6.6 slice-start
  601.4 6.6 slice-start.1
  608.8 52.2 %copy-start.23 = (f32[8,1536]{1,0:T(8,128)}, f32[8,1536]{1,0:T(8,128)S(1)}, u32[]{:S(2)}) copy-start(f32[8,1536]{1,0:T(8,128)S(1)} %get-tuple-element.1037) | copy-start | bytes 147460
  610.2 46.5 %copy-start.30 = (f32[8,12]{1,0:T(8,128)S(1)}, f32[8,12]{1,0:T(8,128)}, u32[]{:S(2)}) copy-start(f32[8,12]{1,0:T(8,128)} %copy-done.29) | copy-start | bytes 1156
  610.2 46.5 %copy-start.31 = (f32[8,12]{1,0:T(8,128)S(1)}, f32[8,12]{1,0:T(8,128)}, u32[]{:S(2)}) copy-start(f32[8,12]{1,0:T(8,128)} %convert_reduce_fusion.5) | copy-start | bytes 1156
  656.4 4.6 copy-start.36
  656.7 39.3 %copy-start.2 = (bf16[1536,288]{0,1:T(8,128)(2,1)S(1)}, bf16[1536,288]{0,1:T(8,128)(2,1)}, u32[]{:S(2)}) copy-start(bf16[1536,288]{0,1:T(8,128)(2,1)} %param.41) | copy-start | bytes 2654212
  657.8 43.4 %copy-start.4 = (bf16[1536,288]{0,1:T(8,128)(2,1)S(1)}, bf16[1536,288]{0,1:T(8,128)(2,1)}, u32[]{:S(2)}) copy-start(bf16[1536,288]{0,1:T(8,128)(2,1)} %param.42) | copy-start | bytes 2654212
  661.0 17.3 %copy-start.25 = (f32[8,1536]{1,0:T(8,128)}, f32[8,1536]{1,0:T(8,128)S(1)}, u32[]{:S(2)}) copy-start(f32[8,1536]{1,0:T(8,128)S(1)} %get-tuple-element.1035) | copy-start | bytes 147460
  661.8 58.5 %copy-start.3 = (bf16[1536,288]{0,1:T(8,128)(2,1)S(1)}, bf16[1536,288]{0,1:T(8,128)(2,1)}, u32[]{:S(2)}) copy-start(bf16[1536,288]{0,1:T(8,128)(2,1)} %param.41) | copy-start | bytes 2654212
  701.2 21.4 %copy-start.28 = (bf16[8,1536]{1,0:T(8,128)(2,1)S(1)}, bf16[8,1536]{1,0:T(8,128)(2,1)}, u32[]{:S(2)}) copy-start(bf16[8,1536]{1,0:T(8,128)(2,1)} %get-tuple-element.988) | copy-start | bytes 73732
  720.7 22.1 %copy-start.43 = (u32[128]{0:T(128)S(1)}, u32[128]{0:T(128)}, u32[]{:S(2)}) copy-start(u32[128]{0:T(128)} %constant.568) | copy-start | bytes 1540
  720.7 23.3 %copy-start.41 = (s32[8]{0:T(128)S(1)}, s32[8]{0:T(128)}, u32[]{:S(2)}) copy-start(s32[8]{0:T(128)} %get-tuple-element.1040) | copy-start | bytes 100
  720.7 23.3 %copy-start.39 = (s32[8]{0:T(128)S(1)}, s32[8]{0:T(128)}, u32[]{:S(2)}) copy-start(s32[8]{0:T(128)} %copy-done.38) | copy-start | bytes 100
  720.7 23.3 %copy-start.42 = (s32[8]{0:T(128)S(1)}, s32[8]{0:T(128)}, u32[]{:S(2)}) copy-start(s32[8]{0:T(128)} %get-tuple-element.1038) | copy-start | bytes 100
  720.7 194.2 %copy-start.24 = (f32[8,1536]{1,0:T(8,128)S(1)}, f32[8,1536]{1,0:T(8,128)}, u32[]{:S(2)}) copy-start(f32[8,1536]{1,0:T(8,128)} %copy-done.23) | copy-start | bytes 147460
  720.7 195.0 %copy-start.26 = (f32[8,1536]{1,0:T(8,128)S(1)}, f32[8,1536]{1,0:T(8,128)}, u32[]{:S(2)}) copy-start(f32[8,1536]{1,0:T(8,128)} %copy-done.25) | copy-start | bytes 147460
  919.3 11.4 %all-to-all-start.1 = ((bf16[4,8,1,1536]{3,0,2,1:T(4,128)(2,1)}), bf16[4,8,1,1536]{3,0,2,1:T(4,128)(2,1)S(1)}, u32[]{:S(2)}, u32[]{:S(2)}) async-start(bf16[4,8,1,1536]{3,0,2,1:T(4,128)(2,1)} %bitcast.140), calls=%async_computation.1 | async-start | bytes 196608 | tf_op jit(solution)/shard_map/all_to_all | solution.py:208
  (9 other events, 10.9 us)
Sparse Core Ops, SparseCore 0:
  63.8 97.4 all-gather.10
  163.5 91.9 all-gather.4
  257.7 102.1 all-gather.6
  424.5 152.7 all-gather.8
  742.9 172.0 all-reduce.6
where the time goes:
time: 955 us; the launch traced here: 939 us
  blocking collectives  387 us (41%)
  waiting for transfers between devices  176 us (18%)
  other arithmetic  146 us (15%)
  local copies, waits for them, and re-layouts  144 us (15%)
  matrix products  56.8 us (6%)
  between operations  15.5 us (2%)
  starting transfers between devices  12.6 us (1%)
    unnamed x6, waiting for transfers between devices  171 us
    all_gather x8, blocking collectives, merged_2(): everything = jax.tree.map(lambda part: lax.all_gather(part, axis), array)  165 us
    all_gather x4, blocking collectives, on_device(): lax.all_gather(query, 'kv', axis=0, tiled=True)  79.3 us
    all_gather x4, blocking collectives, on_device(): lax.all_gather(fresh, 'kv', axis=0, tiled=True)  73.6 us
    dynamic_slice x60, local copies, waits for them, and re-layouts, turn(): return combine(so_far, jax.tree.map(lambda part: part[k], everything))  71.7 us
    add x60, other arithmetic, join_parts(): first[2] * scale_first[..., None] + second[2] * scale_second[..., None]  70.3 us
    all_gather x4, blocking collectives, on_device(): lax.all_gather(rms_round(residual, norm_mlp), 'kv', axis=0, tiled=True)  68.5 us
    add x64, other arithmetic, join_parts(): totals = first[1] * scale_first + second[1] * scale_second  53.3 us
  transfers between devices with their start and end apart: 7, of which 2 were waited for; matrix products, arithmetic and copies ran while one was open for 27% of the time, Pallas kernels for 0%

commit v1 on v0

--- a/solution.py
+++ b/solution.py
@@ -8,6 +8,11 @@
 BEAMS = 8
 EPSILON = 1e-06
 NEGATIVE = -1e30
+
+
+def tiled_gather(x, axis, dim):
+    copies = jnp.concatenate([x] * lax.axis_size(axis), axis=dim)
+    return lax.all_to_all(copies, axis, dim, dim, tiled=True)
 
 
 def merged_2(array, axis, combine):
@@ -193,10 +198,7 @@
             + jnp.dot(attended, w_out, preferred_element_type=jnp.float32)
         ).astype(jnp.bfloat16)
         terms = feed_forward(
-            lax.all_gather(rms_round(residual, norm_mlp), "kv", axis=0, tiled=True),
-            w_gate,
-            w_up,
-            w_down,
+            tiled_gather(rms_round(residual, norm_mlp), "kv", 0), w_gate, w_up, w_down
         )
         summed = lax.psum_scatter(
             terms.astype(jnp.bfloat16), "kv", scatter_dimension=0, tiled=True

time: 955 us -> 933 us (0.977)
  blocking collectives: 387 us -> 329 us
  local copies, waits for them, and re-layouts: 144 us -> 164 us
  starting transfers between devices: 12.6 us -> 30.1 us
    all_gather x4 -> x0, blocking collectives: 68.5 us -> none  [on_device(): lax.all_gather(rms_round(residual, norm_mlp), 'kv', axis=0, tiled=True)]
    unnamed x101 -> x159, local copies, waits for them, and re-layouts: 9.75 us -> 28.3 us
    unnamed x6, waiting for transfers between devices: 171 us -> 153 us
    all_to_all x0 -> x4, starting transfers between devices: none -> 17.7 us  [tiled_gather(): return lax.all_to_all(copies, axis, dim, dim, tiled=True)]
    all_gather x4, blocking collectives: 79.3 us -> 91.5 us  [on_device(): lax.all_gather(query, 'kv', axis=0, tiled=True)]
    all_to_all x0 -> x4, waiting for transfers between devices: none -> 12.1 us  [tiled_gather(): return lax.all_to_all(copies, axis, dim, dim, tiled=True)]
  transfers between devices with their start and end apart: 7 -> 11, of which waited for: 2 -> 5; matrix products, arithmetic and copies ran while one was open for 27% -> 31% of each run, Pallas kernels for 0% -> 0%
where the time goes in v1:
time: 933 us; the launch traced here: 917 us
  blocking collectives  329 us (35%)
  waiting for transfers between devices  170 us (18%)
  local copies, waits for them, and re-layouts  164 us (18%)
  other arithmetic  146 us (16%)
  matrix products  59.9 us (6%)
  starting transfers between devices  30.1 us (3%)
  between operations  15.8 us (2%)
    all_gather x8, blocking collectives, merged_2(): everything = jax.tree.map(lambda part: lax.all_gather(part, axis), array)  165 us
    unnamed x6, waiting for transfers between devices  153 us
    all_gather x4, blocking collectives, on_device(): lax.all_gather(query, 'kv', axis=0, tiled=True)  91.5 us
    all_gather x4, blocking collectives, on_device(): lax.all_gather(fresh, 'kv', axis=0, tiled=True)  72.8 us
    dynamic_slice x60, local copies, waits for them, and re-layouts, turn(): return combine(so_far, jax.tree.map(lambda part: part[k], everything))  71.8 us
    add x60, other arithmetic, join_parts(): first[2] * scale_first[..., None] + second[2] * scale_second[..., None]  69.9 us
    add x64, other arithmetic, join_parts(): totals = first[1] * scale_first + second[1] * scale_second  53.3 us
    unnamed x159, local copies, waits for them, and re-layouts  28.3 us
  transfers between devices with their start and end apart: 11, of which 5 were waited for; matrix products, arithmetic and copies ran while one was open for 31% of the time, Pallas kernels for 0%

profile of v1, /device:TPU:1, one launch (start us, length us, event | category | flops | bytes accessed | tf_op | source)
XLA Modules:
  0.0 916.5 jit_solution(632328622568032233)
XLA Ops:
  12.4 5.8 all-to-all-start
  27.1 7.8 gather_fusion.4
  35.9 3.2 convolution_convert_fusion.4
  39.2 20.2 %all_gather.75 = bf16[128,1536]{1,0:T(8,128)(2,1)S(1)} all-gather(bf16[8,1536]{1,0:T(8,128)(2,1)S(1)} %convolution_convert_fusion.4), channel_id=1, replica_groups=mesh['req'=8,'kv'=16] {'kv'}, dimensions={0}, use_global_device_ids=true | all-gather | bytes 417792 | tf_op jit(solution)/shard_map/all_gather | solution.py:170
  64.2 3.1 convolution_convert_fusion.7
  67.3 19.5 %all_gather.60 = bf16[128,1536]{1,0:T(8,128)(2,1)S(1)} all-gather(bf16[8,1536]{1,0:T(8,128)(2,1)S(1)} %convolution_convert_fusion.7), channel_id=1, replica_groups=mesh['req'=8,'kv'=16] {'kv'}, dimensions={0}, use_global_device_ids=true | all-gather | bytes 417792 | tf_op jit(solution)/shard_map/all_gather | solution.py:170
  86.9 2.8 bitcast_reduce_fusion.3
  93.4 3.1 convolution_convert_fusion.6
  96.5 30.3 %all_gather.65 = bf16[128,1536]{1,0:T(8,128)(2,1)S(1)} all-gather(bf16[8,1536]{1,0:T(8,128)(2,1)S(1)} %convolution_convert_fusion.6), channel_id=1, replica_groups=mesh['req'=8,'kv'=16] {'kv'}, dimensions={0}, use_global_device_ids=true | all-gather | bytes 417792 | tf_op jit(solution)/shard_map/all_gather | solution.py:170
  126.9 2.9 bitcast_reduce_fusion.2
  134.4 3.2 convert_reduce_fusion
  138.3 20.3 %all_gather.64 = bf16[128,256]{1,0:T(8,128)(2,1)S(1)} all-gather(bf16[8,256]{1,0:T(8,128)(2,1)S(1)} %convolution_convert_fusion.11), channel_id=1, replica_groups=mesh['req'=8,'kv'=16] {'kv'}, dimensions={0}, use_global_device_ids=true | all-gather | bytes 69632 | tf_op jit(solution)/shard_map/all_gather | solution.py:171
  161.5 15.6 %all_gather.69 = bf16[128,256]{1,0:T(8,128)(2,1)S(1)} all-gather(bf16[8,256]{1,0:T(8,128)(2,1)S(1)} %convolution_convert_fusion.10), channel_id=1, replica_groups=mesh['req'=8,'kv'=16] {'kv'}, dimensions={0}, use_global_device_ids=true | all-gather | bytes 69632 | tf_op jit(solution)/shard_map/all_gather | solution.py:171
  180.1 19.2 %all_gather.74 = bf16[128,256]{1,0:T(8,128)(2,1)S(1)} all-gather(bf16[8,256]{1,0:T(8,128)(2,1)S(1)} %convolution_convert_fusion.9), channel_id=1, replica_groups=mesh['req'=8,'kv'=16] {'kv'}, dimensions={0}, use_global_device_ids=true | all-gather | bytes 69632 | tf_op jit(solution)/shard_map/all_gather | solution.py:171
  202.2 17.7 %all_gather.79 = bf16[128,256]{1,0:T(8,128)(2,1)S(1)} all-gather(bf16[8,256]{1,0:T(8,128)(2,1)S(1)} %convolution_convert_fusion.8), channel_id=1, replica_groups=mesh['req'=8,'kv'=16] {'kv'}, dimensions={0}, use_global_device_ids=true | all-gather | bytes 69632 | tf_op jit(solution)/shard_map/all_gather | solution.py:171
  220.0 3.4 convert_reduce_fusion.3
  223.7 3.3 convert_reduce_fusion.2
  227.4 3.1 convolution_convert_fusion.5
  230.5 21.5 %all_gather.70 = bf16[128,1536]{1,0:T(8,128)(2,1)S(1)} all-gather(bf16[8,1536]{1,0:T(8,128)(2,1)S(1)} %convolution_convert_fusion.5), channel_id=1, replica_groups=mesh['req'=8,'kv'=16] {'kv'}, dimensions={0}, use_global_device_ids=true | all-gather | bytes 417792 | tf_op jit(solution)/shard_map/all_gather | solution.py:170
  260.0 21.0 %all_gather.76 = f32[16,16,8,12]{1,2,3,0:T(8,128)} all-gather(f32[1,16,8,12]{1,2,3,0:T(8,128)S(1)} %copy.375), channel_id=1, replica_groups=mesh['req'=8,'kv'=16] {'kv'}, dimensions={0}, use_global_device_ids=true | all-gather | bytes 104448 | tf_op jit(solution)/shard_map/all_gather | solution.py:19
  281.0 22.5 %all_gather.77 = f32[16,16,8,12]{1,2,3,0:T(8,128)} all-gather(f32[1,16,8,12]{1,2,3,0:T(8,128)S(1)} %copy.378), channel_id=1, replica_groups=mesh['req'=8,'kv'=16] {'kv'}, dimensions={0}, use_global_device_ids=true | all-gather | bytes 104448 | tf_op jit(solution)/shard_map/all_gather | solution.py:19
  303.5 21.2 %all_gather.61 = f32[16,16,8,12]{1,2,3,0:T(8,128)S(1)} all-gather(f32[1,16,8,12]{1,2,3,0:T(8,128)S(1)} %copy.320), channel_id=1, replica_groups=mesh['req'=8,'kv'=16] {'kv'}, dimensions={0}, use_global_device_ids=true | all-gather | bytes 104448 | tf_op jit(solution)/shard_map/all_gather | solution.py:19
  324.7 23.0 %all_gather.62 = f32[16,16,8,12]{1,2,3,0:T(8,128)S(1)} all-gather(f32[1,16,8,12]{1,2,3,0:T(8,128)S(1)} %copy.323), channel_id=1, replica_groups=mesh['req'=8,'kv'=16] {'kv'}, dimensions={0}, use_global_device_ids=true | all-gather | bytes 104448 | tf_op jit(solution)/shard_map/all_gather | solution.py:19
  347.7 18.1 %all_gather.66 = f32[16,16,8,12]{1,2,3,0:T(8,128)S(1)} all-gather(f32[1,16,8,12]{1,2,3,0:T(8,128)S(1)} %copy.341), channel_id=1, replica_groups=mesh['req'=8,'kv'=16] {'kv'}, dimensions={0}, use_global_device_ids=true | all-gather | bytes 104448 | tf_op jit(solution)/shard_map/all_gather | solution.py:19
  365.8 19.6 %all_gather.67 = f32[16,16,8,12]{1,2,3,0:T(8,128)S(1)} all-gather(f32[1,16,8,12]{1,2,3,0:T(8,128)S(1)} %copy.344), channel_id=1, replica_groups=mesh['req'=8,'kv'=16] {'kv'}, dimensions={0}, use_global_device_ids=true | all-gather | bytes 104448 | tf_op jit(solution)/shard_map/all_gather | solution.py:19
  385.4 19.1 %all_gather.71 = f32[16,16,8,12]{1,2,3,0:T(8,128)} all-gather(f32[1,16,8,12]{1,2,3,0:T(8,128)S(1)} %copy.358), channel_id=1, replica_groups=mesh['req'=8,'kv'=16] {'kv'}, dimensions={0}, use_global_device_ids=true | all-gather | bytes 104448 | tf_op jit(solution)/shard_map/all_gather | solution.py:19
  404.5 20.1 %all_gather.72 = f32[16,16,8,12]{1,2,3,0:T(8,128)} all-gather(f32[1,16,8,12]{1,2,3,0:T(8,128)S(1)} %copy.361), channel_id=1, replica_groups=mesh['req'=8,'kv'=16] {'kv'}, dimensions={0}, use_global_device_ids=true | all-gather | bytes 104448 | tf_op jit(solution)/shard_map/all_gather | solution.py:19
  430.9 2.7 fusion.37
  436.9 46.2 %while.83 = (s32[]{:T(128)}, f32[16,8,12]{0,1,2:T(8,128)S(1)}, f32[16,8,12]{0,1,2:T(8,128)S(1)}, f32[16,8,12,128]{3,2,1,0:T(8,128)S(1)}, f32[16,16,8,12]{1,2,3,0...) while((s32[]{:T(128)}, f32[16,8,12]{0,1,2:T(8,128)S(1)}, ...), condition=%wide.region_32.33_spmd, body=%wide.region_31.32_spmd.sunk | while | flops 599045 | bytes 4018327 | solution.py:25
  485.4 46.3 %while.80 = (s32[]{:T(128)}, f32[16,8,12]{0,1,2:T(8,128)S(1)}, f32[16,8,12]{0,1,2:T(8,128)S(1)}, f32[16,8,12,128]{3,2,1,0:T(8,128)S(1)}, f32[16,16,8,12]{1,2,3,0...) while((s32[]{:T(128)}, f32[16,8,12]{0,1,2:T(8,128)S(1)}, ...), condition=%wide.region_7.8_spmd, body=%wide.region_6.7_spmd.sunk | while | flops 599045 | bytes 4018327 | solution.py:25
  535.1 73.3 %while.81 = (s32[]{:T(128)}, f32[16,8,12]{0,1,2:T(8,128)S(1)}, f32[16,8,12]{0,1,2:T(8,128)S(1)}, f32[16,8,12,128]{3,2,1,0:T(8,128)}, f32[16,16,8,12]{1,2,3,0:T(8...) while((s32[]{:T(128)}, f32[16,8,12]{0,1,2:T(8,128)S(1)}, ...), condition=%wide.region_14.15_spmd, body=%wide.region_13.14_spmd.sunk | while | flops 599045 | bytes 4018327 | solution.py:25
  611.6 4.0 multiply_reduce_fusion.3
  615.6 3.8 multiply_reduce_fusion.2
  622.3 46.2 %while.82 = (s32[]{:T(128)}, f32[16,8,12]{0,1,2:T(8,128)S(1)}, f32[16,8,12]{0,1,2:T(8,128)S(1)}, f32[16,8,12,128]{3,2,1,0:T(8,128)S(1)}, f32[16,16,8,12]{1,2,3,0...) while((s32[]{:T(128)}, f32[16,8,12]{0,1,2:T(8,128)S(1)}, ...), condition=%wide.region_23.24_spmd, body=%wide.region_22.23_spmd.sunk | while | flops 599045 | bytes 4018327 | solution.py:25
  669.7 3.3 multiply_reduce_fusion.1
  675.5 3.9 all-to-all-start.4
  698.5 6.7 all-to-all-start.3
  706.2 2.8 convolution_convert_fusion
  709.0 4.1 all-to-all-done.3
  713.1 3.6 all-to-all-start.2
  717.8 2.8 convolution_convert_fusion.1
  720.6 4.1 all-to-all-done.2
  724.6 3.6 all-to-all-start.1
  729.4 2.8 convolution_convert_fusion.2
  732.2 3.9 all-to-all-done.1
  739.6 152.9 %all-reduce.7.cloned.1.call-done = (bf16[128,1536]{1,0:T(8,128)(2,1)}, bf16[128,1536]{1,0:T(8,128)(2,1)}, bf16[128,1536]{1,0:T(8,128)(2,1)}, bf16[128,1536]{1,0:T(8,128)(2,1)}) async-done(((bf16[128,1536]{1,0:T(8,128)(2,1)}, bf16[128,1536]{1,0:T(8,128)(2,1)}, bf16[128,1536]{1,0:T(8,128)(2,1)}, bf16[128,1536]{1,0:T(8,128)(2,1)}), (bf16[128,1536]{1,0:T(8,128)(2,1)}, bf16[128,1536]{1,0:T(8,128)(2,1)}, ...) | async-done | bytes 1572880
  896.9 6.5 all-to-all-start.5
  903.3 5.0 all-to-all-done.5
  (678 shorter events, 312.0 us)
Async XLA Ops:
  6.5 699.7 %copy-start = (bf16[288,1536]{1,0:T(8,128)(2,1)S(1)}, bf16[288,1536]{1,0:T(8,128)(2,1)}, u32[]{:S(2)}) copy-start(bf16[288,1536]{1,0:T(8,128)(2,1)} %param.43) | copy-start | bytes 2654212
  7.4 27.5 %copy-start.39 = (s32[8]{0:T(128)}, s32[8]{0:T(128)S(1)}, u32[]{:S(2)}) copy-start(s32[8]{0:T(128)S(1)} %select_reduce_fusion) | copy-start | bytes 100
  12.4 22.6 %all-to-all-start = ((bf16[4,8,1,1536]{3,0,2,1:T(4,128)(2,1)}), bf16[4,8,1,1536]{3,0,2,1:T(4,128)(2,1)S(1)}, u32[]{:S(2)}, u32[]{:S(2)}) async-start(bf16[4,8,1,1536]{3,0,2,1:T(4,128)(2,1)} %copy.313), calls=%async_computation | async-start | bytes 196608 | tf_op jit(solution)/shard_map/all_to_all | solution.py:144
  18.2 417.3 %all-gather.11.cloned.1.call-start = ((), (), s32[]{:S(2)}) async-start(), calls=%async_computation.9 | async-start | bytes 13369344 | tf_op jit(solution)/shard_map/all_gather | solution.py:19
  27.1 8.8 copy-start.21
  35.7 23.7 %copy-start.5 = (bf16[72,128,256]{2,1,0:T(8,128)(2,1)S(1)}, bf16[72,128,256]{2,1,0:T(8,128)(2,1)}, u32[]{:S(2)}) copy-start(bf16[72,128,256]{2,1,0:T(8,128)(2,1)} %gather_fusion.4) | copy-start | bytes 14155780
  63.9 419.5 %all-gather.5.cloned.1.call-start = ((), (), s32[]{:S(2)}) async-start(), calls=%async_computation.6 | async-start | bytes 13369344 | tf_op jit(solution)/shard_map/all_gather | solution.py:19
  67.3 22.4 %slice-start.2 = ((s8[4718592]{0:T(1024)(128)(4,1)}), s8[4194304]{0:T(1024)(128)(4,1)S(1)}, s32[]{:S(2)}) async-start(s8[4718592]{0:T(1024)(128)(4,1)} %bitcast.607), calls=%async_computation.13 | async-start | bytes 8388608
  86.9 2.8 slice-start.3
  93.1 439.3 %all-gather.7.cloned.1.call-start = ((), (), s32[]{:S(2)}) async-start(), calls=%async_computation.7 | async-start | bytes 13369344 | tf_op jit(solution)/shard_map/all_gather | solution.py:19
  96.5 33.3 %slice-start.4 = ((s8[4718592]{0:T(1024)(128)(4,1)}), s8[4194304]{0:T(1024)(128)(4,1)S(1)}, s32[]{:S(2)}) async-start(s8[4718592]{0:T(1024)(128)(4,1)} %bitcast.610), calls=%async_computation.15 | async-start | bytes 8388608
  126.9 2.9 slice-start.5
  131.0 7.0 copy-start.4
  133.1 487.8 %all-gather.9.cloned.1.call-start = ((), (), s32[]{:S(2)}) async-start(), calls=%async_computation.8 | async-start | bytes 13369344 | tf_op jit(solution)/shard_map/all_gather | solution.py:19
  178.9 246.2 %copy-start.20 = (bf16[128,4,256]{2,1,0:T(4,128)(2,1)}, bf16[128,4,256]{2,1,0:T(4,128)(2,1)S(1)}, u32[]{:S(2)}) copy-start(bf16[128,4,256]{2,1,0:T(4,128)(2,1)S(1)} %scatter.15) | copy-start | bytes 786436
  201.1 226.3 %copy-start.19 = (bf16[128,4,256]{2,1,0:T(4,128)(2,1)}, bf16[128,4,256]{2,1,0:T(4,128)(2,1)S(1)}, u32[]{:S(2)}) copy-start(bf16[128,4,256]{2,1,0:T(4,128)(2,1)S(1)} %scatter.16) | copy-start | bytes 786436
  260.0 168.4 %copy-start.29 = (bf16[128,4,256]{2,1,0:T(4,128)(2,1)}, bf16[128,4,256]{2,1,0:T(4,128)(2,1)S(1)}, u32[]{:S(2)}) copy-start(bf16[128,4,256]{2,1,0:T(4,128)(2,1)S(1)} %scatter.19) | copy-start | bytes 786436
  260.0 170.9 %copy-start.10 = (f32[8,1152,8,12]{1,3,2,0:T(8,128)S(1)}, f32[8,1152,8,12]{1,3,2,0:T(8,128)}, u32[]{:S(2)}) copy-start(f32[8,1152,8,12]{1,3,2,0:T(8,128)} %copy-done.9) | copy-start | bytes 10616836
  324.7 105.3 %copy-start.17 = (f32[16,16,8,12]{1,2,3,0:T(8,128)}, f32[16,16,8,12]{1,2,3,0:T(8,128)S(1)}, u32[]{:S(2)}) copy-start(f32[16,16,8,12]{1,2,3,0:T(8,128)S(1)} %all_gather.61) | copy-start | bytes 294916
  347.7 82.4 %copy-start.18 = (f32[16,16,8,12]{1,2,3,0:T(8,128)}, f32[16,16,8,12]{1,2,3,0:T(8,128)S(1)}, u32[]{:S(2)}) copy-start(f32[16,16,8,12]{1,2,3,0:T(8,128)S(1)} %all_gather.62) | copy-start | bytes 294916
  365.8 63.4 %copy-start.15 = (f32[16,16,8,12]{1,2,3,0:T(8,128)}, f32[16,16,8,12]{1,2,3,0:T(8,128)S(1)}, u32[]{:S(2)}) copy-start(f32[16,16,8,12]{1,2,3,0:T(8,128)S(1)} %all_gather.66) | copy-start | bytes 294916
  385.4 44.7 %copy-start.16 = (f32[16,16,8,12]{1,2,3,0:T(8,128)}, f32[16,16,8,12]{1,2,3,0:T(8,128)S(1)}, u32[]{:S(2)}) copy-start(f32[16,16,8,12]{1,2,3,0:T(8,128)S(1)} %all_gather.67) | copy-start | bytes 294916
  425.3 8.3 copy-start.38
  427.6 7.3 copy-start.30
  485.4 46.6 %copy-start.41 = (f32[8,1,12]{2,1,0:T(1,128)S(1)}, f32[8,1,12]{2,1,0:T(1,128)}, u32[]{:S(2)}) copy-start(f32[8,1,12]{2,1,0:T(1,128)} %fusion.136) | copy-start | bytes 1156
  535.1 73.6 %copy-start.35 = (f32[8,12]{1,0:T(8,128)S(1)}, f32[8,12]{1,0:T(8,128)}, u32[]{:S(2)}) copy-start(f32[8,12]{1,0:T(8,128)} %copy-done.34) | copy-start | bytes 1156
  535.1 73.6 %copy-start.36 = (f32[8,12]{1,0:T(8,128)S(1)}, f32[8,12]{1,0:T(8,128)}, u32[]{:S(2)}) copy-start(f32[8,12]{1,0:T(8,128)} %convert_reduce_fusion.6) | copy-start | bytes 1156
  611.6 7.8 slice-start
  611.6 7.8 slice-start.1
  622.2 46.5 %copy-start.31 = (f32[8,12]{1,0:T(8,128)S(1)}, f32[8,12]{1,0:T(8,128)}, u32[]{:S(2)}) copy-start(f32[8,12]{1,0:T(8,128)} %copy-done.30) | copy-start | bytes 1156
  622.3 46.5 %copy-start.32 = (f32[8,12]{1,0:T(8,128)S(1)}, f32[8,12]{1,0:T(8,128)}, u32[]{:S(2)}) copy-start(f32[8,12]{1,0:T(8,128)} %convert_reduce_fusion.5) | copy-start | bytes 1156
  668.4 4.6 copy-start.37
  669.7 35.5 %copy-start.2 = (bf16[1536,288]{0,1:T(8,128)(2,1)S(1)}, bf16[1536,288]{0,1:T(8,128)(2,1)}, u32[]{:S(2)}) copy-start(bf16[1536,288]{0,1:T(8,128)(2,1)} %param.41) | copy-start | bytes 2654212
  669.7 36.6 %copy-start.3 = (bf16[1536,288]{0,1:T(8,128)(2,1)S(1)}, bf16[1536,288]{0,1:T(8,128)(2,1)}, u32[]{:S(2)}) copy-start(bf16[1536,288]{0,1:T(8,128)(2,1)} %param.42) | copy-start | bytes 2654212
  675.5 22.2 %all-to-all-start.4 = ((bf16[16,8,1536]{2,1,0:T(8,128)(2,1)}), bf16[16,8,1536]{2,1,0:T(8,128)(2,1)S(1)}, u32[]{:S(2)}, u32[]{:S(2)}) async-start(bf16[16,8,1536]{2,1,0:T(8,128)(2,1)} %bitcast.641), calls=%async_computation.4 | async-start | bytes 786432 | tf_op jit(solution)/shard_map/all_to_all | solution.py:15
  698.5 14.6 %all-to-all-start.3 = ((bf16[16,8,1536]{2,1,0:T(8,128)(2,1)}), bf16[16,8,1536]{2,1,0:T(8,128)(2,1)S(1)}, u32[]{:S(2)}, u32[]{:S(2)}) async-start(bf16[16,8,1536]{2,1,0:T(8,128)(2,1)} %bitcast.640), calls=%async_computation.3 | async-start | bytes 786432 | tf_op jit(solution)/shard_map/all_to_all | solution.py:15
  713.1 11.5 %all-to-all-start.2 = ((bf16[16,8,1536]{2,1,0:T(8,128)(2,1)}), bf16[16,8,1536]{2,1,0:T(8,128)(2,1)S(1)}, u32[]{:S(2)}, u32[]{:S(2)}) async-start(bf16[16,8,1536]{2,1,0:T(8,128)(2,1)} %bitcast.639), calls=%async_computation.2 | async-start | bytes 786432 | tf_op jit(solution)/shard_map/all_to_all | solution.py:15
  724.6 11.5 %all-to-all-start.1 = ((bf16[16,8,1536]{2,1,0:T(8,128)(2,1)}), bf16[16,8,1536]{2,1,0:T(8,128)(2,1)S(1)}, u32[]{:S(2)}, u32[]{:S(2)}) async-start(bf16[16,8,1536]{2,1,0:T(8,128)(2,1)} %bitcast.638), calls=%async_computation.1 | async-start | bytes 786432 | tf_op jit(solution)/shard_map/all_to_all | solution.py:15
  728.2 10.2 %copy-start.44 = (u32[128]{0:T(128)S(1)}, u32[128]{0:T(128)}, u32[]{:S(2)}) copy-start(u32[128]{0:T(128)} %constant.568) | copy-start | bytes 1540
  728.2 11.3 %copy-start.42 = (s32[8]{0:T(128)S(1)}, s32[8]{0:T(128)}, u32[]{:S(2)}) copy-start(s32[8]{0:T(128)} %get-tuple-element.1050) | copy-start | bytes 100
  728.2 11.3 %copy-start.40 = (s32[8]{0:T(128)S(1)}, s32[8]{0:T(128)}, u32[]{:S(2)}) copy-start(s32[8]{0:T(128)} %copy-done.39) | copy-start | bytes 100
  728.2 11.3 %copy-start.43 = (s32[8]{0:T(128)S(1)}, s32[8]{0:T(128)}, u32[]{:S(2)}) copy-start(s32[8]{0:T(128)} %get-tuple-element.1048) | copy-start | bytes 100
  728.2 165.8 %copy-start.25 = (f32[8,1536]{1,0:T(8,128)S(1)}, f32[8,1536]{1,0:T(8,128)}, u32[]{:S(2)}) copy-start(f32[8,1536]{1,0:T(8,128)} %get-tuple-element.1039) | copy-start | bytes 147460
  728.2 164.3 %all-reduce.7.cloned.1.call-start = ((), (), s32[]{:S(2)}) async-start(), calls=%async_computation.10 | async-start | bytes 3145728
  729.4 165.4 %copy-start.24 = (f32[8,1536]{1,0:T(8,128)S(1)}, f32[8,1536]{1,0:T(8,128)}, u32[]{:S(2)}) copy-start(f32[8,1536]{1,0:T(8,128)} %get-tuple-element.1033) | copy-start | bytes 147460
  732.2 160.3 %copy-start.26 = (f32[8,1536]{1,0:T(8,128)S(1)}, f32[8,1536]{1,0:T(8,128)}, u32[]{:S(2)}) copy-start(f32[8,1536]{1,0:T(8,128)} %get-tuple-element.1047) | copy-start | bytes 147460
  732.2 161.1 %copy-start.28 = (f32[8,1536]{1,0:T(8,128)S(1)}, f32[8,1536]{1,0:T(8,128)}, u32[]{:S(2)}) copy-start(f32[8,1536]{1,0:T(8,128)} %copy-done.27) | copy-start | bytes 147460
  896.9 11.4 %all-to-all-start.5 = ((bf16[4,8,1,1536]{3,0,2,1:T(4,128)(2,1)}), bf16[4,8,1,1536]{3,0,2,1:T(4,128)(2,1)S(1)}, u32[]{:S(2)}, u32[]{:S(2)}) async-start(bf16[4,8,1,1536]{3,0,2,1:T(4,128)(2,1)} %bitcast.148), calls=%async_computation.5 | async-start | bytes 196608 | tf_op jit(solution)/shard_map/all_to_all | solution.py:210
  (14 other events, 18.6 us)
Sparse Core Ops, SparseCore 0:
  64.0 97.7 all-gather.10
  164.0 91.4 all-gather.4
  257.8 100.7 all-gather.6
  435.0 151.9 all-gather.8
  738.5 153.9 all-reduce.6
